TPU v7x, 32 devices: a whole 2x2x4 slice. The times are simulated.
32 devices in a mesh: dp: 8 (over z, y), feat: 4 (over x, core).
Axes of the slice: x: 2, y: 2, z: 4, core: 2. Of those that a mesh axis runs over, the one named last changes fastest.
Arguments:
- activations: bfloat16 [16384, 2048], P('feat', 'dp'), may hold values from -6 to 6
- cotangent: bfloat16 [16384, 2048], P('feat', 'dp'), may hold values from -6 to 6
- r_mix: bfloat16 [64, 256, 256], P('feat', 'dp'), may hold values from -0.375 to 0.375
- l_mix: bfloat16 [256, 4096], P('feat', 'dp'), may hold values from -0.75 to 0.75
Outputs:
- grad_x: bfloat16 [16384, 2048], P('feat', 'dp')
- grad_r: float32 [64, 256, 256], P('feat', 'dp')
- grad_l: float32 [256, 4096], P('feat', 'dp')
All inputs are finite; a program needn't handle non-finite values.
Results may differ from a plain program's by a relative error of at most 0.0055.
Values may be sent and summed in bfloat16 or wider, within the bound.
No kernel may reach another device: no remote copies, remote signals or barrier semaphores. Data moves between devices by JAX's collectives and lax.ppermute only.
A program may use at most 64 MiB of HBM per device.

v0:
```python
import math
import jax
import jax.numpy as jnp
from jax import lax
from jax.sharding import PartitionSpec as P

BLOCKS = 64
WIDTH = 256


def gelu_tanh(values):
    return jax.nn.gelu(values, approximate=True)


def slope_of(pre_act, upstream):
    _, pullback = jax.vjp(gelu_tanh, pre_act)
    return pullback(upstream.astype(jnp.float32))[0].astype(jnp.bfloat16)


def body(activations, cotangent, r_mix, l_mix):
    tok_count = activations.shape[1]
    local_blocks = activations.shape[0] // WIDTH
    grad_scale = 1.0 / math.sqrt(tok_count * lax.axis_size("dp"))
    r_whole, l_whole = (
        lax.all_gather(r_mix, "dp", axis=1, tiled=True),
        lax.all_gather(l_mix, "dp", axis=1, tiled=True),
    )
    local_cols = l_whole.shape[0]
    l_blocks = l_whole.reshape(local_cols, BLOCKS, BLOCKS)
    x_blocks = activations.reshape(local_blocks, WIDTH, tok_count)
    g_blocks = cotangent.reshape(local_blocks, WIDTH, tok_count)
    mixed_rows = jnp.einsum(
        "bit,bio->bot", x_blocks, r_whole, preferred_element_type=jnp.float32
    ).astype(jnp.bfloat16)
    outgoing = (mixed_rows,)
    parts = (lax.all_to_all(outgoing[0], "feat", split_axis=1, concat_axis=0, tiled=True),)
    columns = parts[0]
    pre_act = jnp.einsum("bst,sbc->cst", columns, l_blocks, preferred_element_type=jnp.float32)
    arrived = (columns, pre_act) + tuple(parts[1:])
    columns = arrived[0]
    pre_act = arrived[1]
    pre_rows = lax.all_to_all(pre_act, "feat", split_axis=0, concat_axis=1, tiled=True)
    slope_rows = slope_of(pre_rows, g_blocks)
    slope_cols = lax.all_to_all(slope_rows, "feat", split_axis=1, concat_axis=0, tiled=True)
    back_cols = jnp.einsum(
        "cst,sbc->bst", slope_cols, l_blocks, preferred_element_type=jnp.float32
    ).astype(jnp.bfloat16)
    l_term = jnp.einsum("bst,cst->sbc", columns, slope_cols, preferred_element_type=jnp.float32)
    l_term = l_term.reshape(local_cols, BLOCKS * BLOCKS) * grad_scale
    back_rows = lax.all_to_all(back_cols, "feat", split_axis=0, concat_axis=1, tiled=True)
    back_rows, through_r = (
        back_rows,
        jnp.einsum("bot,bio->bit", back_rows, r_whole, preferred_element_type=jnp.float32),
    )
    grad_x = (
        (g_blocks.astype(jnp.float32) + through_r)
        .astype(jnp.bfloat16)
        .reshape(local_blocks * WIDTH, tok_count)
    )
    r_term = (
        jnp.einsum("bit,bot->bio", x_blocks, back_rows, preferred_element_type=jnp.float32)
        * grad_scale
    )
    grad_l, grad_r = (
        lax.psum_scatter(l_term, "dp", scatter_dimension=1, tiled=True),
        lax.psum_scatter(r_term, "dp", scatter_dimension=1, tiled=True),
    )
    return (grad_x, grad_r, grad_l)


def solution(mesh):
    placed = (P("feat", "dp"), P("feat", "dp"), P("feat", "dp", None), P("feat", "dp"))
    return jax.shard_map(
        body,
        mesh=mesh,
        in_specs=placed,
        out_specs=(P("feat", "dp"), P("feat", "dp", None), P("feat", "dp")),
        check_vma=False,
    )
```

profile of v0, /device:TPU:0, one launch (start us, length us, event | category | flops | bytes accessed | tf_op | source)
XLA Modules:
  0.0 399.9 jit_solution(9625601833998472881)
XLA Ops:
  7.9 54.3 %all-gather.2.cloned.1.call-done = bf16[16,256,256]{2,1,0:T(8,128)(2,1)} async-done(((bf16[16,32,256]{2,1,0:T(8,128)(2,1)}), bf16[16,256,256]{2,1,0:T(8,128)(2,1)}) %all-gather.2.cloned.1.call-update) | async-done | bytes 2097168 | tf_op jit(solution)/shard_map/all_gather | solution.py:25
  62.2 2.4 convolution_convert_fusion
  64.6 2.5 copy.19
  67.1 4.6 %all-to-all-start = ((bf16[16,256,256]{2,0,1:T(8,128)(2,1)}), bf16[16,256,256]{2,0,1:T(8,128)(2,1)}, u32[]{:S(2)}, u32[]{:S(2)}) async-start(bf16[16,256,256]{2,0,1:T(8,128)(2,1)} %copy.19), calls=%async_computation | async-start | bytes 4194304 | tf_op jit(solution)/shard_map/all_to_all | solution.py:36
  71.7 33.3 %all_gather.7 = bf16[64,4096]{1,0:T(8,128)(2,1)} all-gather(bf16[64,512]{1,0:T(8,128)(2,1)S(1)} %copy-done.5), channel_id=1, replica_groups=mesh['dp'=8,'feat'=4] {'dp'}, dimensions={1}, use_global_device_ids=true | all-gather | bytes 589824 | tf_op jit(solution)/shard_map/all_gather | solution.py:26
  105.0 2.1 reshape.22
  107.1 1.8 copy.20
  109.0 1.3 copy-done.1
  111.0 2.4 copy.22
  113.5 51.1 %all_to_all.72 = f32[64,64,256]{2,1,0:T(8,128)S(1)} all-to-all(f32[64,64,256]{2,1,0:T(8,128)S(1)} %copy.22), channel_id=1, replica_groups=mesh['dp'=8,'feat'=4] {'feat'}, dimensions={0} | all-to-all | bytes 8388608 | tf_op jit(solution)/shard_map/all_to_all | solution.py:42
  166.1 3.3 fusion.6
  169.5 1.2 copy.24
  170.6 28.2 %all_to_all.73 = bf16[16,256,256]{2,0,1:T(8,128)(2,1)S(1)} all-to-all(bf16[16,256,256]{2,0,1:T(8,128)(2,1)S(1)} %copy.24), channel_id=1, replica_groups=mesh['dp'=8,'feat'=4] {'feat'}, dimensions={1} | all-to-all | bytes 4194304 | tf_op jit(solution)/shard_map/all_to_all | solution.py:44
  200.4 1.2 copy.26
  201.6 28.2 %all_to_all.74 = bf16[64,64,256]{2,1,0:T(8,128)(2,1)S(1)} all-to-all(bf16[64,64,256]{2,1,0:T(8,128)(2,1)S(1)} %copy.26), channel_id=1, replica_groups=mesh['dp'=8,'feat'=4] {'feat'}, dimensions={0} | all-to-all | bytes 4194304 | tf_op jit(solution)/shard_map/all_to_all | solution.py:50
  230.0 1.3 copy-done.3
  231.4 2.7 multiply_bitcast_fusion
  234.1 5.5 %copy.28 = f32[16,256,256]{2,0,1:T(8,128)} copy(f32[16,256,256]{1,2,0:T(8,128)} %multiply_bitcast_fusion) | data formatting | bytes 8388608 | tf_op jit(solution)/shard_map/mul | solution.py:61
  239.6 4.2 %convolution_multiply_fusion = f32[64,64,64]{2,1,0:T(8,128)} fusion(bf16[64,64,256]{2,0,1:T(8,128)(2,1)} %bitcast.50, bf16[64,64,256]{2,0,1:T(8,128)(2,1)} %bitcast.52), kind=kOutput, calls=%fused_computation.20 | convolution fusion | flops 134479872 | bytes 5242880 | tf_op jit(solution)/shard_map/bst,cst->sbc/dot_general | solution.py:48
  243.9 3.1 mul.78
  247.0 4.9 %fusion.10 = bf16[16,256,256]{2,1,0:T(8,128)(2,1)} fusion(bf16[16,256,256]{2,1,0:T(8,128)(2,1)} %bitcast.58, bf16[16,256,256]{2,1,0:T(8,128)(2,1)} %all-gather.2.cloned.1.call-done, bf16[16,256,256]{2,1,0:T(8,128)(2,1)} %bitcast.54), kind=kOutput, calls=%fused_computation.15 | convolution fusion | flops 540016640 | bytes 8388608 | tf_op jit(solution)/shard_map/bot,bio->bit/dot_general | solution.py:53
  251.9 73.5 %reduce-scatter.3.cloned.1.call-done = f32[16,32,256]{2,0,1:T(8,128)} async-done(((f32[16,256,256]{2,0,1:T(8,128)}), f32[16,32,256]{2,0,1:T(8,128)}) %reduce-scatter.3.cloned.1.call-update) | async-done | bytes 524304 | tf_op jit(solution)/shard_map/reduce_scatter | solution.py:66
  325.4 2.1 copy.29
  327.6 65.8 %reduce-scatter.5.cloned.1.call-done = f32[64,512]{1,0:T(8,128)} async-done(((f32[64,4096]{1,0:T(8,128)}), f32[64,512]{1,0:T(8,128)}) %reduce-scatter.5.cloned.1.call-update) | async-done | bytes 131088 | tf_op jit(solution)/shard_map/reduce_scatter | solution.py:65
  (22 shorter events, 5.0 us)
Async XLA Ops:
  7.2 55.0 %copy-start = (bf16[4096,256]{1,0:T(8,128)(2,1)S(1)}, bf16[4096,256]{1,0:T(8,128)(2,1)}, u32[]{:S(2)}) copy-start(bf16[4096,256]{1,0:T(8,128)(2,1)} %param.4) | copy-start | bytes 6291460
  7.2 55.0 %all-gather.2.cloned.1.call-start = ((), (), s32[]{:S(2)}) async-start(), calls=%async_computation.6 | async-start | bytes 2359296 | tf_op jit(solution)/shard_map/all_gather | solution.py:25
  67.1 4.6 %copy-start.5 = (bf16[64,512]{1,0:T(8,128)(2,1)S(1)}, bf16[64,512]{1,0:T(8,128)(2,1)}, u32[]{:S(2)}) copy-start(bf16[64,512]{1,0:T(8,128)(2,1)} %param.7) | copy-start | bytes 196612
  67.1 40.0 %all-to-all-start = ((bf16[16,256,256]{2,0,1:T(8,128)(2,1)}), bf16[16,256,256]{2,0,1:T(8,128)(2,1)}, u32[]{:S(2)}, u32[]{:S(2)}) async-start(bf16[16,256,256]{2,0,1:T(8,128)(2,1)} %copy.19), calls=%async_computation | async-start | bytes 4194304 | tf_op jit(solution)/shard_map/all_to_all | solution.py:36
  71.6 253.8 %reduce-scatter.3.cloned.1.call-start = ((), (), s32[]{:S(2)}) async-start(), calls=%async_computation.7 | async-start | bytes 4718592 | tf_op jit(solution)/shard_map/reduce_scatter | solution.py:66
  109.0 1.3 copy-start.1
  164.6 1.6 copy-start.4
  199.1 1.3 copy-start.2
  230.0 1.3 copy-start.3
  239.6 153.8 %reduce-scatter.5.cloned.1.call-start = ((), (), s32[]{:S(2)}) async-start(), calls=%async_computation.8 | async-start | bytes 1179648 | tf_op jit(solution)/shard_map/reduce_scatter | solution.py:65
Sparse Core Ops, SparseCore 0:
  10.2 51.9 all-gather.1
  239.7 85.6 reduce-scatter.2
  329.8 63.5 reduce-scatter.4
where the time goes:
time: 401 us; the launch traced here: 400 us
  waiting for transfers between devices  194 us (48%)
  blocking collectives  141 us (35%)
  local copies, waits for them, and re-layouts  27.3 us (7%)
  matrix products  15.7 us (4%)
  between operations  13.9 us (3%)
  starting transfers between devices  4.69 us (1%)
    reduce_scatter x1, waiting for transfers between devices, body(): lax.psum_scatter(r_term, 'dp', scatter_dimension=1, tiled=True)  73.5 us
    reduce_scatter x1, waiting for transfers between devices, body(): lax.psum_scatter(l_term, 'dp', scatter_dimension=1, tiled=True)  65.8 us
    all_gather x1, waiting for transfers between devices, body(): lax.all_gather(r_mix, 'dp', axis=1, tiled=True)  54.3 us
    all_to_all x1, blocking collectives, body(): lax.all_to_all(pre_act, 'feat', split_axis=0, concat_axis=1, tiled=True)  51.1 us
    all_gather x1, blocking collectives, body(): lax.all_gather(l_mix, 'dp', axis=1, tiled=True)  33.3 us
    all_to_all x1, blocking collectives, body(): lax.all_to_all(slope_rows, 'feat', split_axis=1, concat_axis=0, tiled=True)  28.2 us
    all_to_all x1, blocking collectives, body(): lax.all_to_all(back_cols, 'feat', split_axis=0, concat_axis=1, tiled=True)  28.2 us
  transfers between devices with their start and end apart: 4, of which 3 were waited for; matrix products, arithmetic and copies ran while one was open for 4% of the time, Pallas kernels for 0%

commit v1 on v0

--- a/solution.py
+++ b/solution.py
@@ -39,7 +39,10 @@
     arrived = (columns, pre_act) + tuple(parts[1:])
     columns = arrived[0]
     pre_act = arrived[1]
-    pre_rows = lax.all_to_all(pre_act, "feat", split_axis=0, concat_axis=1, tiled=True)
+    part_now = lax.all_to_all(
+        jnp.stack(jnp.split(pre_act, lax.axis_size("feat"), 0), 0), "feat", 0, 0
+    )
+    pre_rows = jnp.concatenate(part_now, 1)
     slope_rows = slope_of(pre_rows, g_blocks)
     slope_cols = lax.all_to_all(slope_rows, "feat", split_axis=1, concat_axis=0, tiled=True)
     back_cols = jnp.einsum(

time: 401 us -> 400 us (level)
  no operation moved by 1% of the time
where the time goes in v1:
time: 400 us
  waiting for transfers between devices  194 us (48%)
  blocking collectives  141 us (35%)
  local copies, waits for them, and re-layouts  23.9 us (6%)
  matrix products  15.7 us (4%)
  between operations  13.9 us (3%)
  other arithmetic  6.18 us (2%)
  starting transfers between devices  4.71 us (1%)
    reduce_scatter x1, waiting for transfers between devices, body(): lax.psum_scatter(r_term, 'dp', scatter_dimension=1, tiled=True)  73.6 us
    reduce_scatter x1, waiting for transfers between devices, body(): lax.psum_scatter(l_term, 'dp', scatter_dimension=1, tiled=True)  65.9 us
    all_gather x1, waiting for transfers between devices, body(): lax.all_gather(r_mix, 'dp', axis=1, tiled=True)  54.3 us
    all_to_all x1, blocking collectives, body(): lax.all_to_all(jnp.stack(jnp.split(pre_act, lax.axis_size('feat'), 0), 0)...  51.2 us
    all_gather x1, blocking collectives, body(): lax.all_gather(l_mix, 'dp', axis=1, tiled=True)  33.3 us
    all_to_all x1, blocking collectives, body(): lax.all_to_all(slope_rows, 'feat', split_axis=1, concat_axis=0, tiled=True)  28.2 us
    all_to_all x1, blocking collectives, body(): lax.all_to_all(back_cols, 'feat', split_axis=0, concat_axis=1, tiled=True)  28.2 us
  transfers between devices with their start and end apart: 4, of which 3 were waited for; matrix products, arithmetic and copies ran while one was open for 4% of the time, Pallas kernels for 0%

profile of v1, /device:TPU:0, one launch (start us, length us, event | category | flops | bytes accessed | tf_op | source)
XLA Modules:
  0.0 399.7 jit_solution(11556318988327105060)
XLA Ops:
  7.9 54.3 %all-gather.2.cloned.1.call-done = bf16[16,256,256]{2,1,0:T(8,128)(2,1)} async-done(((bf16[16,32,256]{2,1,0:T(8,128)(2,1)}), bf16[16,256,256]{2,1,0:T(8,128)(2,1)}) %all-gather.2.cloned.1.call-update) | async-done | bytes 2097168 | tf_op jit(solution)/shard_map/all_gather | solution.py:25
  62.2 2.4 convolution_convert_fusion
  64.6 2.5 copy.27
  67.1 4.6 %all-to-all-start = ((bf16[16,256,256]{2,0,1:T(8,128)(2,1)}), bf16[16,256,256]{2,0,1:T(8,128)(2,1)}, u32[]{:S(2)}, u32[]{:S(2)}) async-start(bf16[16,256,256]{2,0,1:T(8,128)(2,1)} %copy.27), calls=%async_computation | async-start | bytes 4194304 | tf_op jit(solution)/shard_map/all_to_all | solution.py:36
  71.7 33.3 %all_gather.7 = bf16[64,4096]{1,0:T(8,128)(2,1)} all-gather(bf16[64,512]{1,0:T(8,128)(2,1)S(1)} %copy-done.5), channel_id=1, replica_groups=mesh['dp'=8,'feat'=4] {'dp'}, dimensions={1}, use_global_device_ids=true | all-gather | bytes 589824 | tf_op jit(solution)/shard_map/all_gather | solution.py:26
  105.1 2.1 reshape.28
  107.1 1.8 copy.28
  109.0 1.3 copy-done.1
  110.3 0.8 convolution_bitcast_fusion
  112.1 51.2 %all_to_all.59 = f32[4,16,64,256]{3,1,2,0:T(8,128)S(1)} all-to-all(f32[4,16,64,256]{3,1,2,0:T(8,128)S(1)} %pad_maximum_fusion), channel_id=1, replica_groups=mesh['dp'=8,'feat'=4] {'feat'}, dimensions={0} | all-to-all | bytes 8388608 | tf_op jit(solution)/shard_map/all_to_all | solution.py:42
  163.3 5.7 %fusion.6 = bf16[16,256,256]{2,1,0:T(8,128)(2,1)S(1)} fusion(bf16[16,256,256]{2,1,0:T(8,128)(2,1)S(1)} %bitcast.59, f32[16,256,256]{2,0,1:T(8,128)S(1)} %bitcast.55), kind=kLoop, calls=%fused_computation.11 | loop fusion | flops 22020096 | bytes 8388608 | tf_op jit(solution)/shard_map/convert_element_type | solution.py:17
  169.1 1.2 copy.35
  170.3 28.2 %all_to_all.60 = bf16[16,256,256]{2,0,1:T(8,128)(2,1)S(1)} all-to-all(bf16[16,256,256]{2,0,1:T(8,128)(2,1)S(1)} %copy.35), channel_id=1, replica_groups=mesh['dp'=8,'feat'=4] {'feat'}, dimensions={1} | all-to-all | bytes 4194304 | tf_op jit(solution)/shard_map/all_to_all | solution.py:47
  200.0 1.2 copy.37
  201.2 28.2 %all_to_all.61 = bf16[64,64,256]{2,1,0:T(8,128)(2,1)S(1)} all-to-all(bf16[64,64,256]{2,1,0:T(8,128)(2,1)S(1)} %copy.37), channel_id=1, replica_groups=mesh['dp'=8,'feat'=4] {'feat'}, dimensions={0} | all-to-all | bytes 4194304 | tf_op jit(solution)/shard_map/all_to_all | solution.py:53
  229.7 1.3 copy-done.3
  231.0 2.7 multiply_bitcast_fusion
  233.7 5.5 %copy.39 = f32[16,256,256]{2,0,1:T(8,128)} copy(f32[16,256,256]{1,2,0:T(8,128)} %multiply_bitcast_fusion) | data formatting | bytes 8388608 | tf_op jit(solution)/shard_map/mul | solution.py:64
  239.2 4.2 %convolution_multiply_fusion = f32[64,64,64]{2,1,0:T(8,128)} fusion(bf16[64,64,256]{2,0,1:T(8,128)(2,1)} %bitcast.50, bf16[64,64,256]{2,0,1:T(8,128)(2,1)} %bitcast.52), kind=kOutput, calls=%fused_computation.21 | convolution fusion | flops 134479872 | bytes 5242880 | tf_op jit(solution)/shard_map/bst,cst->sbc/dot_general | solution.py:51
  243.5 3.1 mul.78
  246.6 4.9 %fusion.10 = bf16[16,256,256]{2,1,0:T(8,128)(2,1)} fusion(bf16[16,256,256]{2,1,0:T(8,128)(2,1)} %bitcast.58, bf16[16,256,256]{2,1,0:T(8,128)(2,1)} %all-gather.2.cloned.1.call-done, bf16[16,256,256]{2,1,0:T(8,128)(2,1)} %bitcast.54), kind=kOutput, calls=%fused_computation.15 | convolution fusion | flops 540016640 | bytes 8388608 | tf_op jit(solution)/shard_map/bot,bio->bit/dot_general | solution.py:56
  251.5 73.6 %reduce-scatter.3.cloned.1.call-done = f32[16,32,256]{2,0,1:T(8,128)} async-done(((f32[16,256,256]{2,0,1:T(8,128)}), f32[16,32,256]{2,0,1:T(8,128)}) %reduce-scatter.3.cloned.1.call-update) | async-done | bytes 524304 | tf_op jit(solution)/shard_map/reduce_scatter | solution.py:69
  325.1 2.1 copy.40
  327.2 65.9 %reduce-scatter.5.cloned.1.call-done = f32[64,512]{1,0:T(8,128)} async-done(((f32[64,4096]{1,0:T(8,128)}), f32[64,512]{1,0:T(8,128)}) %reduce-scatter.5.cloned.1.call-update) | async-done | bytes 131088 | tf_op jit(solution)/shard_map/reduce_scatter | solution.py:68
  (22 shorter events, 3.7 us)
Async XLA Ops:
  7.2 55.0 %copy-start = (bf16[4096,256]{1,0:T(8,128)(2,1)S(1)}, bf16[4096,256]{1,0:T(8,128)(2,1)}, u32[]{:S(2)}) copy-start(bf16[4096,256]{1,0:T(8,128)(2,1)} %param.4) | copy-start | bytes 6291460
  7.2 55.0 %all-gather.2.cloned.1.call-start = ((), (), s32[]{:S(2)}) async-start(), calls=%async_computation.6 | async-start | bytes 2359296 | tf_op jit(solution)/shard_map/all_gather | solution.py:25
  67.1 4.7 %copy-start.5 = (bf16[64,512]{1,0:T(8,128)(2,1)S(1)}, bf16[64,512]{1,0:T(8,128)(2,1)}, u32[]{:S(2)}) copy-start(bf16[64,512]{1,0:T(8,128)(2,1)} %param.7) | copy-start | bytes 196612
  67.1 40.1 %all-to-all-start = ((bf16[16,256,256]{2,0,1:T(8,128)(2,1)}), bf16[16,256,256]{2,0,1:T(8,128)(2,1)}, u32[]{:S(2)}, u32[]{:S(2)}) async-start(bf16[16,256,256]{2,0,1:T(8,128)(2,1)} %copy.27), calls=%async_computation | async-start | bytes 4194304 | tf_op jit(solution)/shard_map/all_to_all | solution.py:36
  71.7 253.4 %reduce-scatter.3.cloned.1.call-start = ((), (), s32[]{:S(2)}) async-start(), calls=%async_computation.7 | async-start | bytes 4718592 | tf_op jit(solution)/shard_map/reduce_scatter | solution.py:69
  109.0 1.3 copy-start.1
  112.1 51.2 %copy-start.4 = (bf16[4096,256]{1,0:T(8,128)(2,1)S(1)}, bf16[4096,256]{1,0:T(8,128)(2,1)}, u32[]{:S(2)}) copy-start(bf16[4096,256]{1,0:T(8,128)(2,1)} %param.5) | copy-start | bytes 6291460
  198.7 1.3 copy-start.2
  229.6 1.3 copy-start.3
  239.2 154.0 %reduce-scatter.5.cloned.1.call-start = ((), (), s32[]{:S(2)}) async-start(), calls=%async_computation.8 | async-start | bytes 1179648 | tf_op jit(solution)/shard_map/reduce_scatter | solution.py:68
Sparse Core Ops, SparseCore 0:
  10.2 51.9 all-gather.1
  239.3 85.7 reduce-scatter.2
  329.5 63.6 reduce-scatter.4
